TPU v7x, 32 devices: a whole 2x2x4 slice. The times are simulated.
32 devices in a mesh: ctx: 8 (over y, x, core), uly: 4 (over z).
Axes of the slice: x: 2, y: 2, z: 4, core: 2. Of those that a mesh axis runs over, the one named last changes fastest.
Arguments:
- query_states: bfloat16 [1024, 2048], P(('ctx', 'uly')), may hold values from -8 to 8
- key_states: bfloat16 [1024, 2048], P(('ctx', 'uly')), may hold values from -8 to 8
- value_states: bfloat16 [1024, 2048], P(('ctx', 'uly')), may hold values from -6 to 6
- score_kernel: float32 [16, 6, 11], P('uly'), may hold values from -0.4 to 1.2
- head_mixing: float32 [16, 4], P('uly'), may hold values from 0.25 to 1
- head_gain: float32 [2048], P('uly'), may hold values from 0.5 to 1.5
Outputs:
- attended: bfloat16 [1024, 2048], P(('ctx', 'uly'))
All inputs are finite; a program needn't handle non-finite values.
Results may differ from a plain program's by a relative error of at most 0.0049.
Values may be sent and summed in bfloat16 or wider, within the bound.
No kernel may reach another device: no remote copies, remote signals or barrier semaphores. Data moves between devices by JAX's collectives and lax.ppermute only.
A program may use at most 64 MiB of HBM per device.

v0:
```python
import jax
import jax.numpy as jnp
from jax import lax
from jax.sharding import PartitionSpec as P

GROUP = 4
QCONV = 6
KCONV = 11
KEY_BLOCK = 128
ROW_CHUNK = 128
KEY_GROUP = 8
lowest = -1e30
epsilon = 1e-06


def passed_along(shard, axis, by):
    peers = lax.axis_size(axis)
    pairs = [(i, i + by) for i in range(peers) if 0 <= i + by < peers]
    return lax.ppermute(shard, axis, pairs)


def split_bf16(values):
    high = lax.reduce_precision(values, exponent_bits=8, mantissa_bits=7)
    low = values - high
    return (high.astype(jnp.bfloat16), low.astype(jnp.bfloat16))


def toeplitz_terms(score_kernel, head_dim):
    col_lead = KCONV - 1
    scaled = score_kernel * head_dim ** (-0.5)
    lag = (
        lax.iota(jnp.int32, KEY_BLOCK)[:, None]
        + col_lead
        - lax.iota(jnp.int32, KEY_BLOCK + col_lead)[None, :]
    )
    toeplitz = jnp.zeros(score_kernel.shape[:2] + lag.shape, jnp.float32)
    for col_lag in range(KCONV):
        toeplitz = jnp.where(lag == col_lag, scaled[:, :, col_lag, None, None], toeplitz)
    return split_bf16(toeplitz)


def convolved_keys(key_windows, terms):
    high, low = terms
    heads = high.shape[0]
    key_heads = key_windows.reshape(key_windows.shape[:2] + (heads, -1))
    conv_keys = jnp.einsum(
        "harc,nchd->nhard", high, key_heads, preferred_element_type=jnp.float32
    ) + jnp.einsum("harc,nchd->nhard", low, key_heads, preferred_element_type=jnp.float32)
    return split_bf16(conv_keys)


def band_terms(query_rows, query_first, key_flat, score_kernel):
    row_lead = QCONV - 1
    heads = score_kernel.shape[0]
    ext_count = query_rows.shape[0]
    row_count = ext_count - row_lead
    near = lax.dynamic_slice_in_dim(key_flat, query_first + 4, ext_count + QCONV - 2, 0)
    query_heads = query_rows.reshape(ext_count, heads, -1).astype(jnp.float32)
    near_heads = near.reshape(near.shape[0], heads, -1).astype(jnp.float32)
    scale = query_heads.shape[2] ** (-0.5)
    diagonals = [
        jnp.sum(query_heads * near_heads[lag - 1 : lag - 1 + ext_count], axis=2) * scale
        for lag in range(1, QCONV)
    ]
    band = []
    for gap in range(QCONV - 1):
        acc = jnp.zeros((row_count, heads), jnp.float32)
        for row_lag in range(gap + 1, QCONV):
            for col_lag in range(row_lag - gap):
                lag = row_lag - col_lag - gap
                acc = (
                    acc
                    - score_kernel[None, :, row_lag, col_lag]
                    * diagonals[lag - 1][row_lead - row_lag : row_lead - row_lag + row_count]
                )
        band.append(acc.T)
    return jnp.stack(band)


def group_logits(shifted, key_windows, terms):
    keys_high, keys_low = convolved_keys(key_windows, terms)
    return jnp.einsum(
        "ihad,nhard->hinr", shifted, keys_high, preferred_element_type=jnp.float32
    ) + jnp.einsum("ihad,nhard->hinr", shifted, keys_low, preferred_element_type=jnp.float32)


def attend_chunk(shifted, band, query_first, key_windows, terms, value_heads, head_mixing):
    row_count, heads = shifted.shape[:2]
    seq_len = value_heads.shape[0]
    window_count = key_windows.shape[0]
    if window_count <= KEY_GROUP:
        convolved = group_logits(shifted, key_windows, terms)
    else:
        grouped_windows = key_windows.reshape(
            (window_count // KEY_GROUP, KEY_GROUP) + key_windows.shape[1:]
        )
        convolved = lax.map(lambda windows: group_logits(shifted, windows, terms), grouped_windows)
        convolved = jnp.moveaxis(convolved, 0, 2)
    convolved = convolved.reshape(heads, row_count, seq_len)
    query_pos = query_first + lax.iota(jnp.int32, row_count)
    gap = query_pos[:, None] - lax.iota(jnp.int32, seq_len)[None, :]
    for lag in range(QCONV - 1):
        convolved = convolved + jnp.where(gap == lag, band[lag][:, :, None], 0.0)
    logits = jnp.where(gap >= 0, convolved, lowest)
    peak = jnp.max(logits, axis=2, keepdims=True)
    expd = jnp.exp(logits - peak)
    probabilities = expd / jnp.sum(expd, axis=2, keepdims=True)
    grouped = probabilities.reshape(heads // GROUP, GROUP, row_count, seq_len)
    weights = head_mixing.reshape(heads // GROUP, GROUP, GROUP)
    mixed_probs = jnp.zeros_like(grouped)
    for source in range(GROUP):
        mixed_probs = mixed_probs + weights[:, :, source, None, None] * grouped[:, source, None]
    mixed_probs = mixed_probs.reshape(heads, row_count, seq_len).astype(jnp.bfloat16)
    return jnp.einsum("hik,khd->ihd", mixed_probs, value_heads, preferred_element_type=jnp.float32)


def normalize(weighted, gain_local):
    factor = lax.rsqrt(jnp.mean(weighted * weighted, axis=2, keepdims=True) + epsilon)
    return (
        (weighted * factor * gain_local[None]).astype(jnp.bfloat16).reshape(weighted.shape[0], -1)
    )


def shards(query_states, key_states, value_states, score_kernel, head_mixing, head_gain):
    stacked = jnp.stack([query_states, key_states, value_states])
    query_local, key_local, value_local = lax.all_to_all(
        stacked, "uly", split_axis=2, concat_axis=1, tiled=True
    )
    shard_rows = query_local.shape[0]
    width = query_local.shape[1]
    row_lead = QCONV - 1
    col_lead = KCONV - 1
    heads = score_kernel.shape[0]
    head_dim = width // heads
    ctx_place = lax.axis_index("ctx")
    query_first = ctx_place * shard_rows
    earlier = passed_along(query_local[shard_rows - row_lead :], "ctx", 1)
    query_ext = jnp.concatenate([earlier, query_local], axis=0)
    key_all, value_all = lax.all_gather(
        jnp.stack([key_local, value_local]), "ctx", axis=1, tiled=True
    )
    seq_len = key_all.shape[0]
    key_pad = jnp.concatenate([jnp.zeros((col_lead, width), key_all.dtype), key_all], axis=0)
    key_windows = jnp.stack(
        [key_pad[start : start + KEY_BLOCK + col_lead] for start in range(0, seq_len, KEY_BLOCK)]
    )
    terms = toeplitz_terms(score_kernel, head_dim)
    edge = jnp.zeros((8, width), key_all.dtype)
    key_flat = jnp.concatenate([edge, key_all, edge], axis=0)
    band = band_terms(query_ext, query_first, key_flat, score_kernel)
    query_heads = query_ext.reshape(shard_rows + row_lead, heads, head_dim)
    shifted = jnp.stack(
        [query_heads[row_lead - lag : row_lead - lag + shard_rows] for lag in range(QCONV)], axis=2
    )
    value_heads = value_all.reshape(seq_len, heads, head_dim)
    chunk = min(ROW_CHUNK * KEY_BLOCK * 8 // seq_len, shard_rows)
    if chunk == shard_rows:
        weighted = attend_chunk(
            shifted, band, query_first, key_windows, terms, value_heads, head_mixing
        )
    else:
        chunks = shard_rows // chunk

        def one_chunk(index):
            start = index * chunk
            return attend_chunk(
                lax.dynamic_slice_in_dim(shifted, start, chunk, 0),
                lax.dynamic_slice_in_dim(band, start, chunk, 2),
                query_first + start,
                key_windows,
                terms,
                value_heads,
                head_mixing,
            )

        weighted = lax.map(one_chunk, jnp.arange(chunks, dtype=jnp.int32))
        weighted = weighted.reshape((shard_rows,) + weighted.shape[2:])
    gain_local = head_gain.reshape(heads, head_dim)
    attended = normalize(weighted, gain_local)
    return lax.all_to_all(attended, "uly", split_axis=0, concat_axis=1, tiled=True)


def solution(mesh):
    placed = (
        P(("ctx", "uly"), None),
        P(("ctx", "uly"), None),
        P(("ctx", "uly"), None),
        P("uly", None, None),
        P("uly", None),
        P("uly"),
    )
    return jax.shard_map(
        shards, mesh=mesh, in_specs=placed, out_specs=P(("ctx", "uly"), None), check_vma=False
    )
```

profile of v0, /device:TPU:0, one launch (start us, length us, event | category | flops | bytes accessed | tf_op | source)
XLA Modules:
  0.0 156.9 jit_solution(3671239521716522393)
XLA Ops:
  6.5 1.1 pad_maximum_fusion
  7.6 1.4 copy.223
  9.0 1.6 %reshape.295 = bf16[4,2,24576]{2,1,0:T(2,128)(2,1)S(1)} reshape(bf16[2048,3,32]{2,1,0:T(4,128)(2,1)S(1)} %bitcast.118) | data formatting | bytes 786432
  10.6 17.8 %all_to_all.34 = bf16[4,2,24576]{2,1,0:T(2,128)(2,1)S(1)} all-to-all(bf16[4,2,24576]{2,1,0:T(2,128)(2,1)S(1)} %reshape.295), channel_id=1, replica_groups=mesh['ctx'=8,'uly'=4] {'uly'}, dimensions={0} | all-to-all | bytes 786432 | tf_op jit(solution)/shard_map/all_to_all | solution.py:126
  28.4 1.3 reshape.296
  29.7 1.2 copy.282
  31.1 0.8 pad_maximum_fusion.1
  32.5 0.7 copy.255
  37.2 0.7 slice_reduce_fusion.18
  38.0 1.0 slice_reduce_fusion.17
  39.0 0.8 fusion.108
  39.7 1.2 fusion.84
  41.0 1.2 subtract_compare_fusion.5
  42.3 1.3 collective-permute-start
  43.6 0.7 concatenate.20
  46.6 12.5 %all-gather.2.cloned.1.call-done = bf16[2,1024,512]{2,1,0:T(8,128)(2,1)} async-done(((bf16[2,128,512]{2,1,0:T(8,128)(2,1)}), bf16[2,1024,512]{2,1,0:T(8,128)(2,1)}) %all-gather.2.cloned.1.call-update) | async-done | bytes 2097168 | tf_op jit(solution)/shard_map/all_gather | solution.py:139
  59.1 1.7 %slice_bitcast_fusion = (bf16[1024,512]{1,0:T(8,128)(2,1)S(1)}, bf16[1,1024,512]{2,1,0:T(8,128)(2,1)S(1)}) fusion(bf16[2,1024,512]{2,1,0:T(8,128)(2,1)} %all-gather.2.cloned.1.call-done), kind=kLoop, calls=%fused_computation.39 | loop fusion | bytes 4194304 | tf_op jit(solution)/shard_map/unstack | solution.py:139
  60.8 0.7 pad_slice_fusion
  61.5 1.6 %stack.75 = bf16[1,138,4,128]{3,2,1,0:T(4,128)(2,1)} reshape(bf16[138,512]{1,0:T(8,128)(2,1)} %pad_slice_fusion) | data formatting | bytes 282624 | tf_op jit(solution)/shard_map/stack | solution.py:144
  63.1 1.6 %copy_dynamic-update-slice_fusion.7 = bf16[8,138,4,128]{3,1,0,2:T(8,128)(2,1)} fusion(bf16[1,138,4,128]{3,2,1,0:T(4,128)(2,1)} %stack.75), kind=kLoop, calls=%fused_computation.138 | loop fusion | bytes 288768
  64.7 2.4 %fusion.127 = (bf16[1,138,512]{2,1,0:T(8,128)(2,1)}, bf16[1,138,512]{2,1,0:T(8,128)(2,1)}, bf16[1,138,512]{2,1,0:T(8,128)(2,1)}, bf16[1,138,512]{2,1,0:T(8,128)(...) fusion(bf16[2,1024,512]{2,1,0:T(8,128)(2,1)} %all-gather.2.cloned.1.call-done), kind=kLoop, calls=%fused_computation.217 | loop fusion | bytes 1978368 | tf_op jit(solution)/shard_map/slice | solution.py:145
  67.1 1.6 %stack.76 = bf16[1,138,4,128]{3,2,1,0:T(4,128)(2,1)} reshape(bf16[1,138,512]{2,1,0:T(8,128)(2,1)} %get-tuple-element.39) | data formatting | bytes 282624 | tf_op jit(solution)/shard_map/stack | solution.py:144
  68.7 1.6 %stack.77 = bf16[1,138,4,128]{3,2,1,0:T(4,128)(2,1)} reshape(bf16[1,138,512]{2,1,0:T(8,128)(2,1)} %get-tuple-element.38) | data formatting | bytes 282624 | tf_op jit(solution)/shard_map/stack | solution.py:144
  70.3 1.6 %stack.78 = bf16[1,138,4,128]{3,2,1,0:T(4,128)(2,1)} reshape(bf16[1,138,512]{2,1,0:T(8,128)(2,1)} %get-tuple-element.37) | data formatting | bytes 282624 | tf_op jit(solution)/shard_map/stack | solution.py:144
  71.9 1.6 %stack.79 = bf16[1,138,4,128]{3,2,1,0:T(4,128)(2,1)} reshape(bf16[1,138,512]{2,1,0:T(8,128)(2,1)} %get-tuple-element.36) | data formatting | bytes 282624 | tf_op jit(solution)/shard_map/stack | solution.py:144
  73.5 1.6 %stack.80 = bf16[1,138,4,128]{3,2,1,0:T(4,128)(2,1)} reshape(bf16[1,138,512]{2,1,0:T(8,128)(2,1)} %get-tuple-element.35) | data formatting | bytes 282624 | tf_op jit(solution)/shard_map/stack | solution.py:144
  75.1 1.6 %stack.81 = bf16[1,138,4,128]{3,2,1,0:T(4,128)(2,1)} reshape(bf16[1,138,512]{2,1,0:T(8,128)(2,1)} %get-tuple-element.34) | data formatting | bytes 282624 | tf_op jit(solution)/shard_map/stack | solution.py:144
  76.7 1.6 %stack.82 = bf16[1,138,4,128]{3,2,1,0:T(4,128)(2,1)} reshape(bf16[1,138,512]{2,1,0:T(8,128)(2,1)} %get-tuple-element.33) | data formatting | bytes 282624 | tf_op jit(solution)/shard_map/stack | solution.py:144
  78.3 1.6 %copy_dynamic-update-slice_fusion.6 = bf16[8,138,4,128]{3,1,0,2:T(8,128)(2,1)} fusion(bf16[8,138,4,128]{3,1,0,2:T(8,128)(2,1)} %copy_dynamic-update-slice_fusion.7, bf16[1,138,4,128]{3,2,1,0:T(4,128)(2,1)} %stack.76), kind=kLoop, calls=%fused_computation.137 | loop fusion | bytes 288768
  79.9 1.6 %copy_dynamic-update-slice_fusion.5 = bf16[8,138,4,128]{3,1,0,2:T(8,128)(2,1)} fusion(bf16[8,138,4,128]{3,1,0,2:T(8,128)(2,1)} %copy_dynamic-update-slice_fusion.6, bf16[1,138,4,128]{3,2,1,0:T(4,128)(2,1)} %stack.77), kind=kLoop, calls=%fused_computation.136 | loop fusion | bytes 288768
  81.5 1.6 %copy_dynamic-update-slice_fusion.4 = bf16[8,138,4,128]{3,1,0,2:T(8,128)(2,1)} fusion(bf16[8,138,4,128]{3,1,0,2:T(8,128)(2,1)} %copy_dynamic-update-slice_fusion.5, bf16[1,138,4,128]{3,2,1,0:T(4,128)(2,1)} %stack.78), kind=kLoop, calls=%fused_computation.135 | loop fusion | bytes 288768
  83.1 1.6 %copy_dynamic-update-slice_fusion.3 = bf16[8,138,4,128]{3,1,0,2:T(8,128)(2,1)} fusion(bf16[8,138,4,128]{3,1,0,2:T(8,128)(2,1)} %copy_dynamic-update-slice_fusion.4, bf16[1,138,4,128]{3,2,1,0:T(4,128)(2,1)} %stack.79), kind=kLoop, calls=%fused_computation.134 | loop fusion | bytes 288768
  84.7 1.6 %copy_dynamic-update-slice_fusion.2 = bf16[8,138,4,128]{3,1,0,2:T(8,128)(2,1)} fusion(bf16[8,138,4,128]{3,1,0,2:T(8,128)(2,1)} %copy_dynamic-update-slice_fusion.3, bf16[1,138,4,128]{3,2,1,0:T(4,128)(2,1)} %stack.80), kind=kLoop, calls=%fused_computation.133 | loop fusion | bytes 288768
  86.3 1.6 %copy_dynamic-update-slice_fusion.1 = bf16[8,138,4,128]{3,1,0,2:T(8,128)(2,1)} fusion(bf16[8,138,4,128]{3,1,0,2:T(8,128)(2,1)} %copy_dynamic-update-slice_fusion.2, bf16[1,138,4,128]{3,2,1,0:T(4,128)(2,1)} %stack.81), kind=kLoop, calls=%fused_computation.132 | loop fusion | bytes 288768
  87.9 1.6 %copy_dynamic-update-slice_fusion = bf16[8,138,4,128]{3,1,0,2:T(8,128)(2,1)} fusion(bf16[8,138,4,128]{3,1,0,2:T(8,128)(2,1)} %copy_dynamic-update-slice_fusion.1, bf16[1,138,4,128]{3,2,1,0:T(4,128)(2,1)} %stack.82), kind=kLoop, calls=%fused_computation.131 | loop fusion | bytes 288768 | tf_op jit(solution)/shard_map/stack | solution.py:144
  89.6 8.7 %fusion.17 = f32[4,8,128,6,128]{4,2,3,1,0:T(8,128)} fusion(bf16[8,138,4,128]{3,1,0,2:T(8,128)(2,1)} %copy_dynamic-update-slice_fusion, f32[4,6]{1,0:T(4,128)S(1)} %bitcast.135, f32[4,6]{1,0:T(4,128)S(1)} %bitcast.137, f32[4,6]{1,0:T(4,128)S(1)} %bitcast.139, f32[4,6]{1,0:T(4,128)S(1)} %bitcast.141, f32[4,6]{1,0:T(4,128)} %bitcast.143, ...), kind=kOutput, calls=%fused_computation.32 | convolution fusion | flops 873732096 | bytes 13908768 | tf_op jit(solution)/shard_map/harc,nchd->nhard/dot_general | solution.py:46
  98.5 6.3 %fusion.15 = f32[4,8,128,6,128]{4,2,3,1,0:T(8,128)} fusion(bf16[8,138,4,128]{3,1,0,2:T(8,128)(2,1)S(1)} %copy-done, f32[4,6]{1,0:T(4,128)S(1)} %bitcast.136, f32[4,6]{1,0:T(4,128)S(1)} %bitcast.138, f32[4,6]{1,0:T(4,128)S(1)} %bitcast.140, f32[4,6]{1,0:T(4,128)S(1)} %bitcast.142, f32[4,6]{1,0:T(4,128)S(1)} %bitcast.144, f32[4,6]{1,0:T(4,128)S(1)} %bitcast.146, ...), kind=kOutput, calls=%fused_computation.30 | convolution fusion | flops 874156032 | bytes 13908768 | tf_op jit(solution)/shard_map/harc,nchd->nhard/dot_general | solution.py:48
  104.8 1.4 copy.227
  107.2 0.8 fusion.90
  108.6 10.9 %fusion.1 = f32[4,128,8,128,1]{1,3,4,2,0:T(8,128)S(1)} fusion(f32[4,8,128,6,128]{4,2,3,1,0:T(8,128)} %fusion.17, f32[4,8,128,6,128]{4,2,3,1,0:T(8,128)} %fusion.15, bf16[128,4,6,128]{3,0,2,1:T(8,128)(2,1)S(1)} %constant_dynamic-update-slice_fusion), kind=kOutput, calls=%fused_computation.3 | convolution fusion | flops 817889280 | bytes 28049408 | tf_op jit(solution)/shard_map/ihad,nhard->hinr/dot_general | solution.py:84
  119.9 10.4 %fusion.85 = (f32[4,128]{1,0:T(4,128)S(1)}, f32[4,128,8,128]{1,3,2,0:T(8,128)S(1)}) fusion(f32[4,128]{1,0:T(4,128)S(1)} %get-tuple-element.74, pred[128,8,128]{0,2,1:T(8,128)(4,1)S(1)} %get-tuple-element.69, f32[4,128]{1,0:T(4,128)S(1)} %get-tuple-element.67, pred[128,8,128]{0,2,1:T(8,128)(4,1)S(1)} %get-tuple-element.70, ...), kind=kOutput, calls=%fused_computation.115 | convolution fusion | flops 821558784 | bytes 30945280 | tf_op jit(solution)/shard_map/ihad,nhard->hinr/dot_general | solution.py:82
  130.4 1.3 exponential_reduce_fusion
  131.7 1.3 fusion.13
  133.1 1.0 copy.271
  134.1 1.0 copy.270
  135.2 1.0 copy.269
  136.5 1.8 %multiply_reduce_fusion = (f32[128,4]{0,1:T(4,128)S(1)}, f32[128,4,128]{0,2,1:T(8,128)S(1)}) fusion(bf16[1024,4,128]{0,2,1:T(8,128)(2,1)S(1)} %bitcast.123, f32[128,1024]{1,0:T(8,128)S(1)} %copy-done.3, f32[4]{0:T(128)S(1)} %copy-done.50, f32[128,1024]{1,0:T(8,128)S(1)} %copy-done.4, f32[4]{0:T(128)S(1)} %copy-done.51, f32[128,1024]{1,0:T(8,128)} %copy.269, ...), kind=kOutput, calls=%fused_computation.127 | convolution fusion | flops 138542592 | bytes 3409984 | tf_op jit(solution)/shard_map/hik,khd->ihd/dot_general | solution.py:114
  138.7 10.7 %all_to_all.35 = bf16[4,32,512]{2,1,0:T(8,128)(2,1)S(1)} all-to-all(bf16[4,32,512]{2,1,0:T(8,128)(2,1)S(1)} %all_to_all.28), channel_id=1, replica_groups=mesh['ctx'=8,'uly'=4] {'uly'}, dimensions={0} | all-to-all | bytes 262144 | tf_op jit(solution)/shard_map/all_to_all | solution.py:180
  (174 shorter events, 10.3 us)
Async XLA Ops:
  6.5 52.5 %all-gather.2.cloned.1.call-start = ((), (), s32[]{:S(2)}) async-start(), calls=%async_computation.2 | async-start | bytes 2359296 | tf_op jit(solution)/shard_map/all_gather | solution.py:139
  29.7 2.2 %copy-start.23 = (f32[4,6,11]{2,0,1:T(4,128)S(1)}, f32[4,6,11]{2,0,1:T(4,128)}, u32[]{:S(2)}) copy-start(f32[4,6,11]{2,0,1:T(4,128)} %param.9) | copy-start | bytes 3172
  29.7 7.5 %copy-start.31 = (f32[4,4]{1,0:T(4,128)S(1)}, f32[4,4]{1,0:T(4,128)}, u32[]{:S(2)}) copy-start(f32[4,4]{1,0:T(4,128)} %param.10) | copy-start | bytes 196
  42.3 2.1 %collective-permute-start = (bf16[5,512]{1,0:T(8,128)(2,1)S(1)}, bf16[5,512]{1,0:T(8,128)(2,1)S(1)}, u32[]{:S(2)}, u32[]{:S(2)}) collective-permute-start(bf16[5,512]{1,0:T(8,128)(2,1)S(1)} %slice.356), channel_id=1, source_target_pairs={{0,4},{4,8},{8,12},{12,16},{16,20},{20,24},{24,28},{1,5},{5,9},{9,... | collective-permute-start | bytes 15368 | tf_op jit(solution)/shard_map/ppermute | solution.py:19
  89.5 8.9 %copy-start = (bf16[8,138,4,128]{3,1,0,2:T(8,128)(2,1)S(1)}, bf16[8,138,4,128]{3,1,0,2:T(8,128)(2,1)}, u32[]{:S(2)}) copy-start(bf16[8,138,4,128]{3,1,0,2:T(8,128)(2,1)} %copy_dynamic-update-slice_fusion) | copy-start | bytes 3391492
  89.5 8.9 %copy-start.12 = (pred[128,138]{0,1:T(8,128)(4,1)S(1)}, pred[128,138]{0,1:T(8,128)(4,1)}, u32[]{:S(2)}) copy-start(pred[128,138]{0,1:T(8,128)(4,1)} %get-tuple-element.81) | copy-start | bytes 52996
  89.5 8.9 %copy-start.13 = (pred[128,138]{0,1:T(8,128)(4,1)S(1)}, pred[128,138]{0,1:T(8,128)(4,1)}, u32[]{:S(2)}) copy-start(pred[128,138]{0,1:T(8,128)(4,1)} %get-tuple-element.82) | copy-start | bytes 52996
  89.5 8.9 %copy-start.14 = (pred[128,138]{0,1:T(8,128)(4,1)S(1)}, pred[128,138]{0,1:T(8,128)(4,1)}, u32[]{:S(2)}) copy-start(pred[128,138]{0,1:T(8,128)(4,1)} %get-tuple-element.83) | copy-start | bytes 52996
  89.5 8.9 %copy-start.15 = (pred[128,138]{0,1:T(8,128)(4,1)S(1)}, pred[128,138]{0,1:T(8,128)(4,1)}, u32[]{:S(2)}) copy-start(pred[128,138]{0,1:T(8,128)(4,1)} %get-tuple-element.84) | copy-start | bytes 52996
  89.5 8.9 %copy-start.16 = (pred[128,138]{0,1:T(8,128)(4,1)S(1)}, pred[128,138]{0,1:T(8,128)(4,1)}, u32[]{:S(2)}) copy-start(pred[128,138]{0,1:T(8,128)(4,1)} %get-tuple-element.85) | copy-start | bytes 52996
  89.5 8.9 %copy-start.17 = (pred[128,138]{0,1:T(8,128)(4,1)S(1)}, pred[128,138]{0,1:T(8,128)(4,1)}, u32[]{:S(2)}) copy-start(pred[128,138]{0,1:T(8,128)(4,1)} %get-tuple-element.86) | copy-start | bytes 52996
  89.5 8.9 %copy-start.18 = (pred[128,138]{0,1:T(8,128)(4,1)S(1)}, pred[128,138]{0,1:T(8,128)(4,1)}, u32[]{:S(2)}) copy-start(pred[128,138]{0,1:T(8,128)(4,1)} %get-tuple-element.87) | copy-start | bytes 52996
  89.5 8.9 %copy-start.19 = (pred[128,138]{0,1:T(8,128)(4,1)S(1)}, pred[128,138]{0,1:T(8,128)(4,1)}, u32[]{:S(2)}) copy-start(pred[128,138]{0,1:T(8,128)(4,1)} %get-tuple-element.88) | copy-start | bytes 52996
  89.5 8.9 %copy-start.20 = (pred[128,138]{0,1:T(8,128)(4,1)S(1)}, pred[128,138]{0,1:T(8,128)(4,1)}, u32[]{:S(2)}) copy-start(pred[128,138]{0,1:T(8,128)(4,1)} %get-tuple-element.89) | copy-start | bytes 52996
  89.5 8.9 %copy-start.21 = (pred[128,138]{0,1:T(8,128)(4,1)S(1)}, pred[128,138]{0,1:T(8,128)(4,1)}, u32[]{:S(2)}) copy-start(pred[128,138]{0,1:T(8,128)(4,1)} %get-tuple-element.90) | copy-start | bytes 52996
  89.6 8.9 %copy-start.22 = (pred[128,138]{0,1:T(8,128)(4,1)S(1)}, pred[128,138]{0,1:T(8,128)(4,1)}, u32[]{:S(2)}) copy-start(pred[128,138]{0,1:T(8,128)(4,1)} %get-tuple-element.91) | copy-start | bytes 52996
  89.6 8.9 %copy-start.24 = (f32[4,6,1]{1,0,2:T(4,128)S(1)}, f32[4,6,1]{1,0,2:T(4,128)}, u32[]{:S(2)}) copy-start(f32[4,6,1]{1,0,2:T(4,128)} %copy.255) | copy-start | bytes 292
  89.6 8.9 %copy-start.25 = (f32[4,6,1]{1,0,2:T(4,128)S(1)}, f32[4,6,1]{1,0,2:T(4,128)}, u32[]{:S(2)}) copy-start(f32[4,6,1]{1,0,2:T(4,128)} %copy.254) | copy-start | bytes 292
  89.6 8.9 %copy-start.26 = (f32[4,6,1]{1,0,2:T(4,128)S(1)}, f32[4,6,1]{1,0,2:T(4,128)}, u32[]{:S(2)}) copy-start(f32[4,6,1]{1,0,2:T(4,128)} %copy.253) | copy-start | bytes 292
  89.6 8.9 %copy-start.27 = (f32[4,6,1]{1,0,2:T(4,128)S(1)}, f32[4,6,1]{1,0,2:T(4,128)}, u32[]{:S(2)}) copy-start(f32[4,6,1]{1,0,2:T(4,128)} %copy.252) | copy-start | bytes 292
  89.6 8.9 %copy-start.28 = (f32[4,6,1]{1,0,2:T(4,128)S(1)}, f32[4,6,1]{1,0,2:T(4,128)}, u32[]{:S(2)}) copy-start(f32[4,6,1]{1,0,2:T(4,128)} %copy.251) | copy-start | bytes 292
  89.6 8.9 %copy-start.29 = (f32[4,6,1]{1,0,2:T(4,128)S(1)}, f32[4,6,1]{1,0,2:T(4,128)}, u32[]{:S(2)}) copy-start(f32[4,6,1]{1,0,2:T(4,128)} %copy.250) | copy-start | bytes 292
  89.6 8.9 %copy-start.30 = (f32[4,6,1]{1,0,2:T(4,128)S(1)}, f32[4,6,1]{1,0,2:T(4,128)}, u32[]{:S(2)}) copy-start(f32[4,6,1]{1,0,2:T(4,128)} %copy.249) | copy-start | bytes 292
  108.4 11.0 %copy-start.33 = (f32[4]{0:T(128)S(1)}, f32[4]{0:T(128)}, u32[]{:S(2)}) copy-start(f32[4]{0:T(128)} %get-tuple-element.11) | copy-start | bytes 52
  108.4 11.0 %copy-start.34 = (f32[4]{0:T(128)S(1)}, f32[4]{0:T(128)}, u32[]{:S(2)}) copy-start(f32[4]{0:T(128)} %get-tuple-element.12) | copy-start | bytes 52
  108.4 11.0 %copy-start.35 = (f32[4]{0:T(128)S(1)}, f32[4]{0:T(128)}, u32[]{:S(2)}) copy-start(f32[4]{0:T(128)} %get-tuple-element.13) | copy-start | bytes 52
  108.5 11.0 %copy-start.36 = (f32[4]{0:T(128)S(1)}, f32[4]{0:T(128)}, u32[]{:S(2)}) copy-start(f32[4]{0:T(128)} %get-tuple-element.16) | copy-start | bytes 52
  108.5 11.0 %copy-start.37 = (f32[4]{0:T(128)S(1)}, f32[4]{0:T(128)}, u32[]{:S(2)}) copy-start(f32[4]{0:T(128)} %get-tuple-element.17) | copy-start | bytes 52
  108.5 11.0 %copy-start.38 = (f32[4]{0:T(128)S(1)}, f32[4]{0:T(128)}, u32[]{:S(2)}) copy-start(f32[4]{0:T(128)} %get-tuple-element.20) | copy-start | bytes 52
  108.5 11.1 %copy-start.39 = (f32[4]{0:T(128)S(1)}, f32[4]{0:T(128)}, u32[]{:S(2)}) copy-start(f32[4]{0:T(128)} %get-tuple-element.15) | copy-start | bytes 52
  108.5 11.1 %copy-start.40 = (f32[4]{0:T(128)S(1)}, f32[4]{0:T(128)}, u32[]{:S(2)}) copy-start(f32[4]{0:T(128)} %get-tuple-element.19) | copy-start | bytes 52
  108.5 11.1 %copy-start.41 = (f32[4]{0:T(128)S(1)}, f32[4]{0:T(128)}, u32[]{:S(2)}) copy-start(f32[4]{0:T(128)} %get-tuple-element.22) | copy-start | bytes 52
  108.5 11.1 %copy-start.42 = (f32[4]{0:T(128)S(1)}, f32[4]{0:T(128)}, u32[]{:S(2)}) copy-start(f32[4]{0:T(128)} %get-tuple-element.24) | copy-start | bytes 52
  108.5 11.2 %copy-start.44 = (f32[4]{0:T(128)S(1)}, f32[4]{0:T(128)}, u32[]{:S(2)}) copy-start(f32[4]{0:T(128)} %get-tuple-element.10) | copy-start | bytes 52
  108.5 11.2 %copy-start.45 = (f32[4]{0:T(128)S(1)}, f32[4]{0:T(128)}, u32[]{:S(2)}) copy-start(f32[4]{0:T(128)} %get-tuple-element.14) | copy-start | bytes 52
  108.5 11.2 %copy-start.46 = (f32[4]{0:T(128)S(1)}, f32[4]{0:T(128)}, u32[]{:S(2)}) copy-start(f32[4]{0:T(128)} %get-tuple-element.18) | copy-start | bytes 52
  108.6 11.2 %copy-start.47 = (f32[4]{0:T(128)S(1)}, f32[4]{0:T(128)}, u32[]{:S(2)}) copy-start(f32[4]{0:T(128)} %get-tuple-element.21) | copy-start | bytes 52
  108.6 11.2 %copy-start.48 = (f32[4]{0:T(128)S(1)}, f32[4]{0:T(128)}, u32[]{:S(2)}) copy-start(f32[4]{0:T(128)} %get-tuple-element.23) | copy-start | bytes 52
  108.6 11.3 %copy-start.1 = (pred[128,8,128]{0,2,1:T(8,128)(4,1)S(1)}, pred[128,8,128]{0,2,1:T(8,128)(4,1)}, u32[]{:S(2)}) copy-start(pred[128,8,128]{0,2,1:T(8,128)(4,1)} %get-tuple-element.73) | copy-start | bytes 393220
  130.3 1.3 copy-start.6
  130.3 1.3 copy-start.7
  133.1 3.3 %copy-start.2 = (bf16[1,1024,512]{1,2,0:T(8,128)(2,1)S(1)}, bf16[1,1024,512]{1,2,0:T(8,128)(2,1)}, u32[]{:S(2)}) copy-start(bf16[1,1024,512]{1,2,0:T(8,128)(2,1)} %copy.227) | copy-start | bytes 3145732
  133.1 3.3 %copy-start.49 = (f32[4]{0:T(128)S(1)}, f32[4]{0:T(128)}, u32[]{:S(2)}) copy-start(f32[4]{0:T(128)} %get-tuple-element.25) | copy-start | bytes 52
  133.1 3.3 %copy-start.50 = (f32[4]{0:T(128)S(1)}, f32[4]{0:T(128)}, u32[]{:S(2)}) copy-start(f32[4]{0:T(128)} %get-tuple-element.26) | copy-start | bytes 52
  133.1 3.3 %copy-start.51 = (f32[4]{0:T(128)S(1)}, f32[4]{0:T(128)}, u32[]{:S(2)}) copy-start(f32[4]{0:T(128)} %get-tuple-element.27) | copy-start | bytes 52
  133.1 3.3 %copy-start.52 = (f32[4]{0:T(128)S(1)}, f32[4]{0:T(128)}, u32[]{:S(2)}) copy-start(f32[4]{0:T(128)} %get-tuple-element.28) | copy-start | bytes 52
  134.1 2.3 %copy-start.3 = (f32[128,1024]{1,0:T(8,128)S(1)}, f32[128,1024]{1,0:T(8,128)}, u32[]{:S(2)}) copy-start(f32[128,1024]{1,0:T(8,128)} %copy.271) | copy-start | bytes 1572868
  136.4 1.9 %copy-start.43 = (f32[512]{0:T(512)S(1)}, f32[512]{0:T(512)}, u32[]{:S(2)}) copy-start(f32[512]{0:T(512)} %param.11) | copy-start | bytes 6148
  (7 other events, 8.4 us)
Sparse Core Ops, SparseCore 0:
  32.0 26.9 all-gather.1
where the time goes:
time: 158 us; the launch traced here: 157 us
  local copies, waits for them, and re-layouts  52.8 us (33%)
  matrix products  38.1 us (24%)
  blocking collectives  28.5 us (18%)
  between operations  14.5 us (9%)
  waiting for transfers between devices  12.6 us (8%)
  other arithmetic  9 us (6%)
    all_to_all x1, blocking collectives, shards(): lax.all_to_all(stacked, 'uly', split_axis=2, concat_axis=1, tiled=True)  17.8 us
    unnamed x121, local copies, waits for them, and re-layouts  14.7 us
    another operation x9, local copies, waits for them, and re-layouts, shards(): jnp.stack([key_pad[start:start + KEY_BLOCK + col_lead] for start in range...  14.4 us
    all_gather x1, waiting for transfers between devices, shards(): lax.all_gather(jnp.stack([key_local, value_local]), 'ctx', axis=1, tiled=...  12.5 us
    dot_general x1, matrix products, group_logits(): jnp.einsum('ihad,nhard->hinr', shifted, keys_low, preferred_element_type=...  10.9 us
    all_to_all x1, blocking collectives, shards(): lax.all_to_all(attended, 'uly', split_axis=0, concat_axis=1, tiled=True)  10.7 us
    dot_general x1, matrix products, group_logits(): jnp.einsum('ihad,nhard->hinr', shifted, keys_high, preferred_element_type...  10.4 us
    dot_general x1, matrix products, convolved_keys(): jnp.einsum('harc,nchd->nhard', high, key_heads, preferred_element_type=jn...  8.7 us
  transfers between devices with their start and end apart: 2, of which 2 were waited for; matrix products, arithmetic and copies ran while one was open for 8% of the time, Pallas kernels for 0%

commit v1 on v0

--- a/solution.py
+++ b/solution.py
@@ -11,6 +11,18 @@
 KEY_GROUP = 8
 lowest = -1e30
 epsilon = 1e-06
+
+
+def resolve_blocks_over_axis(raw, dim_no, page):
+    small = raw.shape
+    seen_now = raw.reshape(*small[:dim_no], page, small[dim_no] // page, *small[dim_no + 1 :])
+    return jnp.moveaxis(seen_now, dim_no, 0)
+
+
+def _mix_marks(local_array, array_axis):
+    field_out = list(local_array.shape[1:])
+    field_out[array_axis] *= local_array.shape[0]
+    return jnp.moveaxis(local_array, 0, array_axis).reshape(field_out)
 
 
 def passed_along(shard, axis, by):
@@ -123,9 +135,24 @@
 
 def shards(query_states, key_states, value_states, score_kernel, head_mixing, head_gain):
     stacked = jnp.stack([query_states, key_states, value_states])
-    query_local, key_local, value_local = lax.all_to_all(
-        stacked, "uly", split_axis=2, concat_axis=1, tiled=True
-    )
+
+    def _show_object(mine_x, along_axis, local_values, unit):
+        long_array = jax.lax.axis_size(along_axis)
+        latest = jax.lax.axis_index(along_axis)
+        carry_out, frame_out = (long_array, latest)
+        view_out = resolve_blocks_over_axis(mine_x, local_values, carry_out)
+        ledger = [view_out[frame_out]]
+        src_i = 1
+        while src_i < carry_out:
+            f_now = view_out[frame_out ^ src_i]
+            reply = jax.lax.ppermute(f_now, along_axis, [(b, b ^ src_i) for b in range(carry_out)])
+            ledger.append(reply)
+            src_i = src_i + 1
+        t1 = jnp.stack(ledger, axis=0)
+        view_out = t1[frame_out ^ jnp.arange(carry_out)]
+        return _mix_marks(view_out, unit)
+
+    query_local, key_local, value_local = _show_object(stacked, "uly", 2, 1)
     shard_rows = query_local.shape[0]
     width = query_local.shape[1]
     row_lead = QCONV - 1

time: 158 us -> 152 us (0.962)
  blocking collectives: 28.5 us -> 10.7 us
  waiting for transfers between devices: 12.6 us -> 21.2 us
  starting transfers between devices: 1.29 us -> 7.1 us
    all_to_all x1 -> x0, blocking collectives: 17.8 us -> none  [shards(): lax.all_to_all(stacked, 'uly', split_axis=2, concat_axis=1, tiled=True)]
    ppermute x0 -> x3, waiting for transfers between devices: none -> 7.47 us  [_show_object(): jax.lax.ppermute(f_now, along_axis, [(b, b ^ src_i) for b in range(carry_...]
    ppermute x0 -> x3, starting transfers between devices: none -> 5.8 us  [_show_object(): jax.lax.ppermute(f_now, along_axis, [(b, b ^ src_i) for b in range(carry_...]
    unnamed x121 -> x125, local copies, waits for them, and re-layouts: 14.7 us -> 12 us
    another operation x1 -> x4, local copies, waits for them, and re-layouts: 1.36 us -> 3.01 us  [shards(): stacked = jnp.stack([query_states, key_states, value_states])]
  transfers between devices with their start and end apart: 2 -> 5, of which waited for: 2 -> 4; matrix products, arithmetic and copies ran while one was open for 8% -> 9% of each run, Pallas kernels for 0% -> 0%
where the time goes in v1:
time: 152 us
  local copies, waits for them, and re-layouts  51.9 us (34%)
  matrix products  38.1 us (25%)
  waiting for transfers between devices  21.2 us (14%)
  between operations  14.6 us (10%)
  blocking collectives  10.7 us (7%)
  other arithmetic  7.98 us (5%)
  starting transfers between devices  7.1 us (5%)
    another operation x9, local copies, waits for them, and re-layouts, shards(): jnp.stack([key_pad[start:start + KEY_BLOCK + col_lead] for start in range...  14.4 us
    all_gather x1, waiting for transfers between devices, shards(): lax.all_gather(jnp.stack([key_local, value_local]), 'ctx', axis=1, tiled=...  13.6 us
    unnamed x125, local copies, waits for them, and re-layouts  12 us
    dot_general x1, matrix products, group_logits(): jnp.einsum('ihad,nhard->hinr', shifted, keys_low, preferred_element_type=...  10.9 us
    all_to_all x1, blocking collectives, shards(): lax.all_to_all(attended, 'uly', split_axis=0, concat_axis=1, tiled=True)  10.7 us
    dot_general x1, matrix products, group_logits(): jnp.einsum('ihad,nhard->hinr', shifted, keys_high, preferred_element_type...  10.4 us
    dot_general x1, matrix products, convolved_keys(): jnp.einsum('harc,nchd->nhard', high, key_heads, preferred_element_type=jn...  8.7 us
    ppermute x3, waiting for transfers between devices, _show_object(): jax.lax.ppermute(f_now, along_axis, [(b, b ^ src_i) for b in range(carry_...  7.47 us
  transfers between devices with their start and end apart: 5, of which 4 were waited for; matrix products, arithmetic and copies ran while one was open for 9% of the time, Pallas kernels for 0%

profile of v1, /device:TPU:0, one launch (start us, length us, event | category | flops | bytes accessed | tf_op | source)
XLA Modules:
  0.0 151.6 jit_solution(224983315837740233)
XLA Ops:
  6.5 1.0 stack.75
  7.6 1.0 stack.76
  8.6 1.0 stack.77
  9.7 0.9 constant_dynamic-slice_fusion.3
  10.7 5.1 %collective-permute-start.2 = (bf16[3,32,512]{2,1,0:T(8,128)(2,1)S(1)}, bf16[3,32,512]{2,1,0:T(8,128)(2,1)S(1)}, u32[]{:S(2)}, u32[]{:S(2)}) collective-permute-start(bf16[3,32,512]{2,1,0:T(8,128)(2,1)S(1)} %bitcast.149), channel_id=1, source_target_pairs={{0,3},{1,2},{2,1},{3,0},{4,7},{5,6},{6,5},{7,4},{8,11},{9,10},{10,... | collective-permute-start | bytes 294920 | tf_op jit(solution)/shard_map/ppermute | solution.py:148
  16.6 2.8 %collective-permute-done.2 = bf16[3,32,512]{2,1,0:T(8,128)(2,1)S(1)} collective-permute-done((bf16[3,32,512]{2,1,0:T(8,128)(2,1)S(1)}, bf16[3,32,512]{2,1,0:T(8,128)(2,1)S(1)}, u32[]{:S(2)}, u32[]{:S(2)}) %collective-permute-start.2) | collective-permute-done | bytes 98336 | tf_op jit(solution)/shard_map/ppermute | solution.py:148
  19.4 4.7 %collective-permute-done.1 = bf16[3,32,512]{2,1,0:T(8,128)(2,1)S(1)} collective-permute-done((bf16[3,32,512]{2,1,0:T(8,128)(2,1)S(1)}, bf16[3,32,512]{2,1,0:T(8,128)(2,1)S(1)}, u32[]{:S(2)}, u32[]{:S(2)}) %collective-permute-start.1) | collective-permute-done | bytes 98336 | tf_op jit(solution)/shard_map/ppermute | solution.py:148
  24.7 0.8 pad_maximum_fusion.1
  30.8 0.7 slice_reduce_fusion.18
  31.6 1.0 slice_reduce_fusion.17
  32.5 0.8 fusion.108
  33.3 1.2 fusion.84
  34.5 1.2 subtract_compare_fusion.5
  35.8 1.3 collective-permute-start.3
  37.1 0.7 concatenate.21
  40.1 13.6 %all-gather.2.cloned.1.call-done = bf16[2,1024,512]{2,1,0:T(8,128)(2,1)} async-done(((bf16[2,128,512]{2,1,0:T(8,128)(2,1)}), bf16[2,1024,512]{2,1,0:T(8,128)(2,1)}) %all-gather.2.cloned.1.call-update) | async-done | bytes 2097168 | tf_op jit(solution)/shard_map/all_gather | solution.py:166
  53.7 1.7 %slice_bitcast_fusion = (bf16[1024,512]{1,0:T(8,128)(2,1)S(1)}, bf16[1,1024,512]{2,1,0:T(8,128)(2,1)S(1)}) fusion(bf16[2,1024,512]{2,1,0:T(8,128)(2,1)} %all-gather.2.cloned.1.call-done), kind=kLoop, calls=%fused_computation.40 | loop fusion | bytes 4194304 | tf_op jit(solution)/shard_map/unstack | solution.py:166
  55.4 0.7 pad_slice_fusion
  56.1 1.6 %stack.91 = bf16[1,138,4,128]{3,2,1,0:T(4,128)(2,1)} reshape(bf16[138,512]{1,0:T(8,128)(2,1)} %pad_slice_fusion) | data formatting | bytes 282624 | tf_op jit(solution)/shard_map/stack | solution.py:171
  57.7 1.6 %copy_dynamic-update-slice_fusion.7 = bf16[8,138,4,128]{3,1,0,2:T(8,128)(2,1)} fusion(bf16[1,138,4,128]{3,2,1,0:T(4,128)(2,1)} %stack.91), kind=kLoop, calls=%fused_computation.139 | loop fusion | bytes 288768
  59.3 2.4 %fusion.128 = (bf16[1,138,512]{2,1,0:T(8,128)(2,1)}, bf16[1,138,512]{2,1,0:T(8,128)(2,1)}, bf16[1,138,512]{2,1,0:T(8,128)(2,1)}, bf16[1,138,512]{2,1,0:T(8,128)(...) fusion(bf16[2,1024,512]{2,1,0:T(8,128)(2,1)} %all-gather.2.cloned.1.call-done), kind=kLoop, calls=%fused_computation.232 | loop fusion | bytes 1978368 | tf_op jit(solution)/shard_map/slice | solution.py:172
  61.7 1.6 %stack.92 = bf16[1,138,4,128]{3,2,1,0:T(4,128)(2,1)} reshape(bf16[1,138,512]{2,1,0:T(8,128)(2,1)} %get-tuple-element.39) | data formatting | bytes 282624 | tf_op jit(solution)/shard_map/stack | solution.py:171
  63.3 1.6 %stack.93 = bf16[1,138,4,128]{3,2,1,0:T(4,128)(2,1)} reshape(bf16[1,138,512]{2,1,0:T(8,128)(2,1)} %get-tuple-element.38) | data formatting | bytes 282624 | tf_op jit(solution)/shard_map/stack | solution.py:171
  64.9 1.6 %stack.94 = bf16[1,138,4,128]{3,2,1,0:T(4,128)(2,1)} reshape(bf16[1,138,512]{2,1,0:T(8,128)(2,1)} %get-tuple-element.37) | data formatting | bytes 282624 | tf_op jit(solution)/shard_map/stack | solution.py:171
  66.5 1.6 %stack.95 = bf16[1,138,4,128]{3,2,1,0:T(4,128)(2,1)} reshape(bf16[1,138,512]{2,1,0:T(8,128)(2,1)} %get-tuple-element.36) | data formatting | bytes 282624 | tf_op jit(solution)/shard_map/stack | solution.py:171
  68.1 1.6 %stack.96 = bf16[1,138,4,128]{3,2,1,0:T(4,128)(2,1)} reshape(bf16[1,138,512]{2,1,0:T(8,128)(2,1)} %get-tuple-element.35) | data formatting | bytes 282624 | tf_op jit(solution)/shard_map/stack | solution.py:171
  69.7 1.6 %stack.97 = bf16[1,138,4,128]{3,2,1,0:T(4,128)(2,1)} reshape(bf16[1,138,512]{2,1,0:T(8,128)(2,1)} %get-tuple-element.34) | data formatting | bytes 282624 | tf_op jit(solution)/shard_map/stack | solution.py:171
  71.3 1.6 %stack.98 = bf16[1,138,4,128]{3,2,1,0:T(4,128)(2,1)} reshape(bf16[1,138,512]{2,1,0:T(8,128)(2,1)} %get-tuple-element.33) | data formatting | bytes 282624 | tf_op jit(solution)/shard_map/stack | solution.py:171
  72.9 1.6 %copy_dynamic-update-slice_fusion.6 = bf16[8,138,4,128]{3,1,0,2:T(8,128)(2,1)} fusion(bf16[8,138,4,128]{3,1,0,2:T(8,128)(2,1)} %copy_dynamic-update-slice_fusion.7, bf16[1,138,4,128]{3,2,1,0:T(4,128)(2,1)} %stack.92), kind=kLoop, calls=%fused_computation.138 | loop fusion | bytes 288768
  74.5 1.6 %copy_dynamic-update-slice_fusion.5 = bf16[8,138,4,128]{3,1,0,2:T(8,128)(2,1)} fusion(bf16[8,138,4,128]{3,1,0,2:T(8,128)(2,1)} %copy_dynamic-update-slice_fusion.6, bf16[1,138,4,128]{3,2,1,0:T(4,128)(2,1)} %stack.93), kind=kLoop, calls=%fused_computation.137 | loop fusion | bytes 288768
  76.1 1.6 %copy_dynamic-update-slice_fusion.4 = bf16[8,138,4,128]{3,1,0,2:T(8,128)(2,1)} fusion(bf16[8,138,4,128]{3,1,0,2:T(8,128)(2,1)} %copy_dynamic-update-slice_fusion.5, bf16[1,138,4,128]{3,2,1,0:T(4,128)(2,1)} %stack.94), kind=kLoop, calls=%fused_computation.136 | loop fusion | bytes 288768
  77.7 1.6 %copy_dynamic-update-slice_fusion.3 = bf16[8,138,4,128]{3,1,0,2:T(8,128)(2,1)} fusion(bf16[8,138,4,128]{3,1,0,2:T(8,128)(2,1)} %copy_dynamic-update-slice_fusion.4, bf16[1,138,4,128]{3,2,1,0:T(4,128)(2,1)} %stack.95), kind=kLoop, calls=%fused_computation.135 | loop fusion | bytes 288768
  79.3 1.6 %copy_dynamic-update-slice_fusion.2 = bf16[8,138,4,128]{3,1,0,2:T(8,128)(2,1)} fusion(bf16[8,138,4,128]{3,1,0,2:T(8,128)(2,1)} %copy_dynamic-update-slice_fusion.3, bf16[1,138,4,128]{3,2,1,0:T(4,128)(2,1)} %stack.96), kind=kLoop, calls=%fused_computation.134 | loop fusion | bytes 288768
  80.9 1.6 %copy_dynamic-update-slice_fusion.1 = bf16[8,138,4,128]{3,1,0,2:T(8,128)(2,1)} fusion(bf16[8,138,4,128]{3,1,0,2:T(8,128)(2,1)} %copy_dynamic-update-slice_fusion.2, bf16[1,138,4,128]{3,2,1,0:T(4,128)(2,1)} %stack.97), kind=kLoop, calls=%fused_computation.133 | loop fusion | bytes 288768
  82.5 1.6 %copy_dynamic-update-slice_fusion = bf16[8,138,4,128]{3,1,0,2:T(8,128)(2,1)} fusion(bf16[8,138,4,128]{3,1,0,2:T(8,128)(2,1)} %copy_dynamic-update-slice_fusion.1, bf16[1,138,4,128]{3,2,1,0:T(4,128)(2,1)} %stack.98), kind=kLoop, calls=%fused_computation.132 | loop fusion | bytes 288768 | tf_op jit(solution)/shard_map/stack | solution.py:171
  84.3 8.7 %fusion.17 = f32[4,8,128,6,128]{4,2,3,1,0:T(8,128)} fusion(bf16[8,138,4,128]{3,1,0,2:T(8,128)(2,1)} %copy_dynamic-update-slice_fusion, f32[4,6]{1,0:T(4,128)S(1)} %bitcast.152, f32[4,6]{1,0:T(4,128)S(1)} %bitcast.154, f32[4,6]{1,0:T(4,128)S(1)} %bitcast.156, f32[4,6]{1,0:T(4,128)S(1)} %bitcast.158, f32[4,6]{1,0:T(4,128)} %bitcast.160, ...), kind=kOutput, calls=%fused_computation.33 | convolution fusion | flops 873732096 | bytes 13908768 | tf_op jit(solution)/shard_map/harc,nchd->nhard/dot_general | solution.py:58
  93.2 6.3 %fusion.15 = f32[4,8,128,6,128]{4,2,3,1,0:T(8,128)} fusion(bf16[8,138,4,128]{3,1,0,2:T(8,128)(2,1)S(1)} %copy-done, f32[4,6]{1,0:T(4,128)S(1)} %bitcast.153, f32[4,6]{1,0:T(4,128)S(1)} %bitcast.155, f32[4,6]{1,0:T(4,128)S(1)} %bitcast.157, f32[4,6]{1,0:T(4,128)S(1)} %bitcast.159, f32[4,6]{1,0:T(4,128)S(1)} %bitcast.161, f32[4,6]{1,0:T(4,128)S(1)} %bitcast.163, ...), kind=kOutput, calls=%fused_computation.31 | convolution fusion | flops 874156032 | bytes 13908768 | tf_op jit(solution)/shard_map/harc,nchd->nhard/dot_general | solution.py:60
  99.5 1.4 copy.151
  101.8 0.8 fusion.90
  103.2 10.9 %fusion.1 = f32[4,128,8,128,1]{1,3,4,2,0:T(8,128)S(1)} fusion(f32[4,8,128,6,128]{4,2,3,1,0:T(8,128)} %fusion.17, f32[4,8,128,6,128]{4,2,3,1,0:T(8,128)} %fusion.15, bf16[128,4,6,128]{3,0,2,1:T(8,128)(2,1)S(1)} %constant_dynamic-update-slice_fusion.3), kind=kOutput, calls=%fused_computation.4 | convolution fusion | flops 817889280 | bytes 28049408 | tf_op jit(solution)/shard_map/ihad,nhard->hinr/dot_general | solution.py:96
  114.5 10.4 %fusion.85 = (f32[4,128]{1,0:T(4,128)S(1)}, f32[4,128,8,128]{1,3,2,0:T(8,128)S(1)}) fusion(f32[4,128]{1,0:T(4,128)S(1)} %get-tuple-element.78, pred[128,8,128]{0,2,1:T(8,128)(4,1)S(1)} %get-tuple-element.73, f32[4,128]{1,0:T(4,128)S(1)} %get-tuple-element.71, pred[128,8,128]{0,2,1:T(8,128)(4,1)S(1)} %get-tuple-element.74, ...), kind=kOutput, calls=%fused_computation.116 | convolution fusion | flops 821558784 | bytes 30945280 | tf_op jit(solution)/shard_map/ihad,nhard->hinr/dot_general | solution.py:94
  125.0 1.3 exponential_reduce_fusion
  126.3 1.2 fusion.13
  127.8 1.0 copy.192
  128.8 1.0 copy.191
  129.8 1.0 copy.190
  131.1 1.8 %multiply_reduce_fusion = (f32[128,4]{0,1:T(4,128)S(1)}, f32[128,4,128]{0,2,1:T(8,128)S(1)}) fusion(bf16[1024,4,128]{0,2,1:T(8,128)(2,1)S(1)} %bitcast.136, f32[128,1024]{1,0:T(8,128)S(1)} %copy-done.3, f32[4]{0:T(128)S(1)} %copy-done.50, f32[128,1024]{1,0:T(8,128)S(1)} %copy-done.4, f32[4]{0:T(128)S(1)} %copy-done.51, f32[128,1024]{1,0:T(8,128)} %copy.190, ...), kind=kOutput, calls=%fused_computation.128 | convolution fusion | flops 138542592 | bytes 3409984 | tf_op jit(solution)/shard_map/hik,khd->ihd/dot_general | solution.py:126
  133.3 10.7 %all_to_all.19 = bf16[4,32,512]{2,1,0:T(8,128)(2,1)S(1)} all-to-all(bf16[4,32,512]{2,1,0:T(8,128)(2,1)S(1)} %all_to_all.14), channel_id=1, replica_groups=mesh['ctx'=8,'uly'=4] {'uly'}, dimensions={0} | all-to-all | bytes 262144 | tf_op jit(solution)/shard_map/all_to_all | solution.py:207
  (186 shorter events, 12.4 us)
Async XLA Ops:
  6.5 47.2 %all-gather.2.cloned.1.call-start = ((), (), s32[]{:S(2)}) async-start(), calls=%async_computation.1 | async-start | bytes 2359296 | tf_op jit(solution)/shard_map/all_gather | solution.py:166
  10.6 14.9 %copy-start.23 = (f32[4,6,11]{2,0,1:T(4,128)S(1)}, f32[4,6,11]{2,0,1:T(4,128)}, u32[]{:S(2)}) copy-start(f32[4,6,11]{2,0,1:T(4,128)} %param.9) | copy-start | bytes 3172
  10.7 8.7 %collective-permute-start.2 = (bf16[3,32,512]{2,1,0:T(8,128)(2,1)S(1)}, bf16[3,32,512]{2,1,0:T(8,128)(2,1)S(1)}, u32[]{:S(2)}, u32[]{:S(2)}) collective-permute-start(bf16[3,32,512]{2,1,0:T(8,128)(2,1)S(1)} %bitcast.149), channel_id=1, source_target_pairs={{0,3},{1,2},{2,1},{3,0},{4,7},{5,6},{6,5},{7,4},{8,11},{9,10},{10,... | collective-permute-start | bytes 294920 | tf_op jit(solution)/shard_map/ppermute | solution.py:148
  15.8 8.2 %collective-permute-start.1 = (bf16[3,32,512]{2,1,0:T(8,128)(2,1)S(1)}, bf16[3,32,512]{2,1,0:T(8,128)(2,1)S(1)}, u32[]{:S(2)}, u32[]{:S(2)}) collective-permute-start(bf16[3,32,512]{2,1,0:T(8,128)(2,1)S(1)} %bitcast.150), channel_id=1, source_target_pairs={{0,2},{1,3},{2,0},{3,1},{4,6},{5,7},{6,4},{7,5},{8,10},{9,11},{10,... | collective-permute-start | bytes 294920 | tf_op jit(solution)/shard_map/ppermute | solution.py:148
  15.9 14.9 %copy-start.31 = (f32[4,4]{1,0:T(4,128)S(1)}, f32[4,4]{1,0:T(4,128)}, u32[]{:S(2)}) copy-start(f32[4,4]{1,0:T(4,128)} %param.10) | copy-start | bytes 196
  15.9 8.1 %collective-permute-start = (bf16[3,32,512]{2,1,0:T(8,128)(2,1)S(1)}, bf16[3,32,512]{2,1,0:T(8,128)(2,1)S(1)}, u32[]{:S(2)}, u32[]{:S(2)}) collective-permute-start(bf16[3,32,512]{2,1,0:T(8,128)(2,1)S(1)} %bitcast.151), channel_id=1, source_target_pairs={{0,1},{1,0},{2,3},{3,2},{4,5},{5,4},{6,7},{7,6},{8,9},{9,8},{10,11... | collective-permute-start | bytes 294920 | tf_op jit(solution)/shard_map/ppermute | solution.py:148
  35.8 2.1 %collective-permute-start.3 = (bf16[5,512]{1,0:T(8,128)(2,1)S(1)}, bf16[5,512]{1,0:T(8,128)(2,1)S(1)}, u32[]{:S(2)}, u32[]{:S(2)}) collective-permute-start(bf16[5,512]{1,0:T(8,128)(2,1)S(1)} %slice.358), channel_id=1, source_target_pairs={{0,4},{4,8},{8,12},{12,16},{16,20},{20,24},{24,28},{1,5},{5,9},{9,... | collective-permute-start | bytes 15368 | tf_op jit(solution)/shard_map/ppermute | solution.py:31
  84.1 8.9 %copy-start = (bf16[8,138,4,128]{3,1,0,2:T(8,128)(2,1)S(1)}, bf16[8,138,4,128]{3,1,0,2:T(8,128)(2,1)}, u32[]{:S(2)}) copy-start(bf16[8,138,4,128]{3,1,0,2:T(8,128)(2,1)} %copy_dynamic-update-slice_fusion) | copy-start | bytes 3391492
  84.1 8.9 %copy-start.12 = (pred[128,138]{0,1:T(8,128)(4,1)S(1)}, pred[128,138]{0,1:T(8,128)(4,1)}, u32[]{:S(2)}) copy-start(pred[128,138]{0,1:T(8,128)(4,1)} %get-tuple-element.85) | copy-start | bytes 52996
  84.1 8.9 %copy-start.13 = (pred[128,138]{0,1:T(8,128)(4,1)S(1)}, pred[128,138]{0,1:T(8,128)(4,1)}, u32[]{:S(2)}) copy-start(pred[128,138]{0,1:T(8,128)(4,1)} %get-tuple-element.86) | copy-start | bytes 52996
  84.1 8.9 %copy-start.14 = (pred[128,138]{0,1:T(8,128)(4,1)S(1)}, pred[128,138]{0,1:T(8,128)(4,1)}, u32[]{:S(2)}) copy-start(pred[128,138]{0,1:T(8,128)(4,1)} %get-tuple-element.87) | copy-start | bytes 52996
  84.1 8.9 %copy-start.15 = (pred[128,138]{0,1:T(8,128)(4,1)S(1)}, pred[128,138]{0,1:T(8,128)(4,1)}, u32[]{:S(2)}) copy-start(pred[128,138]{0,1:T(8,128)(4,1)} %get-tuple-element.88) | copy-start | bytes 52996
  84.1 8.9 %copy-start.16 = (pred[128,138]{0,1:T(8,128)(4,1)S(1)}, pred[128,138]{0,1:T(8,128)(4,1)}, u32[]{:S(2)}) copy-start(pred[128,138]{0,1:T(8,128)(4,1)} %get-tuple-element.89) | copy-start | bytes 52996
  84.2 8.9 %copy-start.17 = (pred[128,138]{0,1:T(8,128)(4,1)S(1)}, pred[128,138]{0,1:T(8,128)(4,1)}, u32[]{:S(2)}) copy-start(pred[128,138]{0,1:T(8,128)(4,1)} %get-tuple-element.90) | copy-start | bytes 52996
  84.2 8.9 %copy-start.18 = (pred[128,138]{0,1:T(8,128)(4,1)S(1)}, pred[128,138]{0,1:T(8,128)(4,1)}, u32[]{:S(2)}) copy-start(pred[128,138]{0,1:T(8,128)(4,1)} %get-tuple-element.91) | copy-start | bytes 52996
  84.2 8.9 %copy-start.19 = (pred[128,138]{0,1:T(8,128)(4,1)S(1)}, pred[128,138]{0,1:T(8,128)(4,1)}, u32[]{:S(2)}) copy-start(pred[128,138]{0,1:T(8,128)(4,1)} %get-tuple-element.92) | copy-start | bytes 52996
  84.2 8.9 %copy-start.20 = (pred[128,138]{0,1:T(8,128)(4,1)S(1)}, pred[128,138]{0,1:T(8,128)(4,1)}, u32[]{:S(2)}) copy-start(pred[128,138]{0,1:T(8,128)(4,1)} %get-tuple-element.93) | copy-start | bytes 52996
  84.2 8.9 %copy-start.21 = (pred[128,138]{0,1:T(8,128)(4,1)S(1)}, pred[128,138]{0,1:T(8,128)(4,1)}, u32[]{:S(2)}) copy-start(pred[128,138]{0,1:T(8,128)(4,1)} %get-tuple-element.94) | copy-start | bytes 52996
  84.2 8.9 %copy-start.22 = (pred[128,138]{0,1:T(8,128)(4,1)S(1)}, pred[128,138]{0,1:T(8,128)(4,1)}, u32[]{:S(2)}) copy-start(pred[128,138]{0,1:T(8,128)(4,1)} %get-tuple-element.95) | copy-start | bytes 52996
  84.2 8.9 %copy-start.24 = (f32[4,6,1]{1,0,2:T(4,128)S(1)}, f32[4,6,1]{1,0,2:T(4,128)}, u32[]{:S(2)}) copy-start(f32[4,6,1]{1,0,2:T(4,128)} %copy.177) | copy-start | bytes 292
  84.2 8.9 %copy-start.25 = (f32[4,6,1]{1,0,2:T(4,128)S(1)}, f32[4,6,1]{1,0,2:T(4,128)}, u32[]{:S(2)}) copy-start(f32[4,6,1]{1,0,2:T(4,128)} %copy.176) | copy-start | bytes 292
  84.2 8.9 %copy-start.26 = (f32[4,6,1]{1,0,2:T(4,128)S(1)}, f32[4,6,1]{1,0,2:T(4,128)}, u32[]{:S(2)}) copy-start(f32[4,6,1]{1,0,2:T(4,128)} %copy.175) | copy-start | bytes 292
  84.2 8.9 %copy-start.27 = (f32[4,6,1]{1,0,2:T(4,128)S(1)}, f32[4,6,1]{1,0,2:T(4,128)}, u32[]{:S(2)}) copy-start(f32[4,6,1]{1,0,2:T(4,128)} %copy.174) | copy-start | bytes 292
  84.3 8.9 %copy-start.28 = (f32[4,6,1]{1,0,2:T(4,128)S(1)}, f32[4,6,1]{1,0,2:T(4,128)}, u32[]{:S(2)}) copy-start(f32[4,6,1]{1,0,2:T(4,128)} %copy.173) | copy-start | bytes 292
  84.3 8.9 %copy-start.29 = (f32[4,6,1]{1,0,2:T(4,128)S(1)}, f32[4,6,1]{1,0,2:T(4,128)}, u32[]{:S(2)}) copy-start(f32[4,6,1]{1,0,2:T(4,128)} %copy.172) | copy-start | bytes 292
  84.3 8.9 %copy-start.30 = (f32[4,6,1]{1,0,2:T(4,128)S(1)}, f32[4,6,1]{1,0,2:T(4,128)}, u32[]{:S(2)}) copy-start(f32[4,6,1]{1,0,2:T(4,128)} %copy.171) | copy-start | bytes 292
  103.1 11.0 %copy-start.33 = (f32[4]{0:T(128)S(1)}, f32[4]{0:T(128)}, u32[]{:S(2)}) copy-start(f32[4]{0:T(128)} %get-tuple-element.11) | copy-start | bytes 52
  103.1 11.0 %copy-start.34 = (f32[4]{0:T(128)S(1)}, f32[4]{0:T(128)}, u32[]{:S(2)}) copy-start(f32[4]{0:T(128)} %get-tuple-element.12) | copy-start | bytes 52
  103.1 11.0 %copy-start.35 = (f32[4]{0:T(128)S(1)}, f32[4]{0:T(128)}, u32[]{:S(2)}) copy-start(f32[4]{0:T(128)} %get-tuple-element.13) | copy-start | bytes 52
  103.1 11.0 %copy-start.36 = (f32[4]{0:T(128)S(1)}, f32[4]{0:T(128)}, u32[]{:S(2)}) copy-start(f32[4]{0:T(128)} %get-tuple-element.16) | copy-start | bytes 52
  103.1 11.0 %copy-start.37 = (f32[4]{0:T(128)S(1)}, f32[4]{0:T(128)}, u32[]{:S(2)}) copy-start(f32[4]{0:T(128)} %get-tuple-element.17) | copy-start | bytes 52
  103.1 11.0 %copy-start.38 = (f32[4]{0:T(128)S(1)}, f32[4]{0:T(128)}, u32[]{:S(2)}) copy-start(f32[4]{0:T(128)} %get-tuple-element.20) | copy-start | bytes 52
  103.1 11.1 %copy-start.39 = (f32[4]{0:T(128)S(1)}, f32[4]{0:T(128)}, u32[]{:S(2)}) copy-start(f32[4]{0:T(128)} %get-tuple-element.15) | copy-start | bytes 52
  103.1 11.1 %copy-start.40 = (f32[4]{0:T(128)S(1)}, f32[4]{0:T(128)}, u32[]{:S(2)}) copy-start(f32[4]{0:T(128)} %get-tuple-element.19) | copy-start | bytes 52
  103.2 11.1 %copy-start.41 = (f32[4]{0:T(128)S(1)}, f32[4]{0:T(128)}, u32[]{:S(2)}) copy-start(f32[4]{0:T(128)} %get-tuple-element.22) | copy-start | bytes 52
  103.2 11.1 %copy-start.42 = (f32[4]{0:T(128)S(1)}, f32[4]{0:T(128)}, u32[]{:S(2)}) copy-start(f32[4]{0:T(128)} %get-tuple-element.24) | copy-start | bytes 52
  103.2 11.2 %copy-start.44 = (f32[4]{0:T(128)S(1)}, f32[4]{0:T(128)}, u32[]{:S(2)}) copy-start(f32[4]{0:T(128)} %get-tuple-element.10) | copy-start | bytes 52
  103.2 11.2 %copy-start.45 = (f32[4]{0:T(128)S(1)}, f32[4]{0:T(128)}, u32[]{:S(2)}) copy-start(f32[4]{0:T(128)} %get-tuple-element.14) | copy-start | bytes 52
  103.2 11.2 %copy-start.46 = (f32[4]{0:T(128)S(1)}, f32[4]{0:T(128)}, u32[]{:S(2)}) copy-start(f32[4]{0:T(128)} %get-tuple-element.18) | copy-start | bytes 52
  103.2 11.2 %copy-start.47 = (f32[4]{0:T(128)S(1)}, f32[4]{0:T(128)}, u32[]{:S(2)}) copy-start(f32[4]{0:T(128)} %get-tuple-element.21) | copy-start | bytes 52
  103.2 11.2 %copy-start.48 = (f32[4]{0:T(128)S(1)}, f32[4]{0:T(128)}, u32[]{:S(2)}) copy-start(f32[4]{0:T(128)} %get-tuple-element.23) | copy-start | bytes 52
  103.2 11.3 %copy-start.1 = (pred[128,8,128]{0,2,1:T(8,128)(4,1)S(1)}, pred[128,8,128]{0,2,1:T(8,128)(4,1)}, u32[]{:S(2)}) copy-start(pred[128,8,128]{0,2,1:T(8,128)(4,1)} %get-tuple-element.77) | copy-start | bytes 393220
  127.7 3.3 %copy-start.2 = (bf16[1,1024,512]{1,2,0:T(8,128)(2,1)S(1)}, bf16[1,1024,512]{1,2,0:T(8,128)(2,1)}, u32[]{:S(2)}) copy-start(bf16[1,1024,512]{1,2,0:T(8,128)(2,1)} %copy.151) | copy-start | bytes 3145732
  127.7 3.3 %copy-start.49 = (f32[4]{0:T(128)S(1)}, f32[4]{0:T(128)}, u32[]{:S(2)}) copy-start(f32[4]{0:T(128)} %get-tuple-element.25) | copy-start | bytes 52
  127.7 3.3 %copy-start.50 = (f32[4]{0:T(128)S(1)}, f32[4]{0:T(128)}, u32[]{:S(2)}) copy-start(f32[4]{0:T(128)} %get-tuple-element.26) | copy-start | bytes 52
  127.8 3.3 %copy-start.51 = (f32[4]{0:T(128)S(1)}, f32[4]{0:T(128)}, u32[]{:S(2)}) copy-start(f32[4]{0:T(128)} %get-tuple-element.27) | copy-start | bytes 52
  127.8 3.3 %copy-start.52 = (f32[4]{0:T(128)S(1)}, f32[4]{0:T(128)}, u32[]{:S(2)}) copy-start(f32[4]{0:T(128)} %get-tuple-element.28) | copy-start | bytes 52
  128.8 2.3 %copy-start.3 = (f32[128,1024]{1,0:T(8,128)S(1)}, f32[128,1024]{1,0:T(8,128)}, u32[]{:S(2)}) copy-start(f32[128,1024]{1,0:T(8,128)} %copy.192) | copy-start | bytes 1572868
  (10 other events, 12.9 us)
Sparse Core Ops, SparseCore 0:
  25.6 28.0 all-gather.1
